TPU v7x, 512 devices: a whole 4x8x8 slice. The times are simulated.
512 devices in a mesh: section: 32 (over z, x), et: 16 (over y, core).
Axes of the slice: x: 4, y: 8, z: 8, core: 2. Of those that a mesh axis runs over, the one named last changes fastest.
Arguments:
- x_fwd: bfloat16 [32, 256, 3072], P('section', 'et'), may hold values from -6 to 6
- act_fwd: bfloat16 [32, 256, 8192], P('section', None, 'et'), may hold values from -6 to 6
- ids_fwd: int32 [32, 256, 2], P('section'), may hold values from 0 to 7, as said below
- x_bwd: bfloat16 [32, 256, 3072], P('section', 'et'), may hold values from -6 to 6
- act_bwd: bfloat16 [32, 256, 8192], P('section', None, 'et'), may hold values from -6 to 6
- ids_bwd: int32 [32, 256, 2], P('section'), may hold values from 0 to 7, as said below
- grad_out: bfloat16 [32, 256, 3072], P('section', 'et'), may hold values from -6 to 6
- gain: bfloat16 [32, 3072], P('section'), may hold values from 0.099609375 to 1.8984375
- w_router: bfloat16 [32, 3072, 8], P('section'), may hold values from -0.21875 to 0.21875
- w_down: bfloat16 [32, 8192, 3072], P('section', 'et'), may hold values from -0.0625 to 0.0625
Outputs:
- fwd_in: bfloat16 [32, 256, 3072], P('section', 'et')
- incoming_gradient: bfloat16 [32, 256, 3072], P('section', 'et')
- dact: bfloat16 [32, 256, 8192], P('section', None, 'et')
Inputs may be any that keep to these rules, and one draw needn't show every extreme that they name: `ids_fwd`: each token names 2 different experts; in each section's micro-batch exactly 128 tokens name expert 0. `ids_bwd`: each token names 2 different experts; in each section's micro-batch exactly 128 tokens name expert 0.
All inputs are finite; a program needn't handle non-finite values.
Results may differ from a plain program's by a relative error of at most 0.014.
Values may be sent and summed in bfloat16 or wider, within the bound.
No kernel may reach another device: no remote copies, remote signals or barrier semaphores. Data moves between devices by JAX's collectives and lax.ppermute only.
A program may use at most 64 MiB of HBM per device.

v0:
```python
import jax
import jax.numpy as jnp
from jax import lax
from jax.sharding import PartitionSpec as P


def from_behind(value, axis, steps):
    count = lax.axis_size(axis)
    first, last = (max(0, -steps), min(count, count - steps))
    return lax.ppermute(value, axis, [(source, source + steps) for source in range(first, last)])


def norm_logits(inputs, gain, w_router):
    wide = inputs.astype(jnp.float32)
    inverse = lax.rsqrt(jnp.mean(wide * wide, axis=-1, keepdims=True) + 1e-05)
    normed = (wide * inverse * gain.astype(jnp.float32)).astype(jnp.bfloat16)
    logits = jnp.dot(normed, w_router, preferred_element_type=jnp.float32).astype(jnp.bfloat16)
    return (wide, inverse, logits)


def routing(logits, chosen, experts):
    route = jnp.sum((chosen == 0).astype(jnp.float32), axis=1)
    partner = jnp.minimum(jnp.sum(chosen, axis=1), experts - 1)
    labels = jnp.arange(experts, dtype=jnp.int32)
    onehot = (partner[:, None] == labels[None, :]).astype(jnp.float32)
    wide_logits = logits.astype(jnp.float32)
    sigma = jax.nn.sigmoid(wide_logits[:, 0] - jnp.sum(wide_logits * onehot, axis=1))
    return (route, onehot, sigma, route * sigma)


def arrange(chosen):
    member = jnp.sum((chosen == 0).astype(jnp.int32), axis=1)
    tally = jnp.sum(member)
    before = jnp.cumsum(member) - member
    after = jnp.cumsum(1 - member) - (1 - member)
    place = jnp.where(member == 1, before, tally + after)
    ordering = jnp.zeros_like(member).at[place].set(jnp.arange(member.shape[0], dtype=jnp.int32))
    return (member, place, ordering)


def spread_back(compact, member, place, capacity):
    safe = jnp.minimum(place, capacity - 1)
    return jnp.where(member[:, None] == 1, compact[safe], 0.0)


def shards(x_fwd, act_fwd, ids_fwd, x_bwd, act_bwd, ids_bwd, grad_out, gain, w_router, w_down):
    x_fwd, act_fwd, ids_fwd, x_bwd, act_bwd = (
        x_fwd[0],
        act_fwd[0],
        ids_fwd[0],
        x_bwd[0],
        act_bwd[0],
    )
    ids_bwd, grad_out, gain, w_router, w_down = (
        ids_bwd[0],
        grad_out[0],
        gain[0],
        w_router[0],
        w_down[0],
    )
    experts = w_router.shape[1]
    tokens = ids_fwd.shape[0]
    capacity = tokens // 2
    own_rows = x_fwd.shape[0]
    first_row = lax.axis_index("et") * own_rows
    wide_f, inverse_f, logit_f = norm_logits(x_fwd, gain, w_router)
    backward_wide_rows, backward_inverse_norm, logit_b = norm_logits(x_bwd, gain, w_router)
    full_f, full_b, full_g = (
        lax.all_gather(logit_f, "et", axis=0, tiled=True),
        lax.all_gather(logit_b, "et", axis=0, tiled=True),
        lax.all_gather(grad_out, "et", axis=0, tiled=True),
    )
    route_f, onehot_f, sigma_f, coef_f = routing(full_f, ids_fwd, experts)
    member_f, place_f, order_f = arrange(ids_fwd)
    chosen_f = order_f[:capacity]
    compact = (
        jnp.dot(act_fwd[chosen_f], w_down, preferred_element_type=jnp.float32)
        * coef_f[chosen_f][:, None]
    )
    summed = lax.psum(compact.astype(jnp.bfloat16), "et").astype(jnp.float32)
    member_own = lax.dynamic_slice_in_dim(member_f, first_row, own_rows, 0)
    place_own = lax.dynamic_slice_in_dim(place_f, first_row, own_rows, 0)
    y_mine = spread_back(summed, member_own, place_own, capacity)
    layer_out = (wide_f + y_mine).astype(jnp.bfloat16)
    route_b, onehot_b, sigma_b, backward_coefficient = routing(full_b, ids_bwd, experts)
    member_b, place_b, order_b = arrange(ids_bwd)
    chosen_b = order_b[:capacity]
    up_compact = lax.dot_general(
        full_g[chosen_b], w_down, (((1,), (1,)), ((), ())), preferred_element_type=jnp.float32
    )
    back_up = spread_back(up_compact, member_b, place_b, capacity)
    dact = (backward_coefficient[:, None] * back_up).astype(jnp.bfloat16)
    dprob_part = jnp.sum(act_bwd.astype(jnp.float32) * back_up, axis=1)
    dprob_all = lax.psum(dprob_part, "et")
    dprob_mine = lax.dynamic_slice_in_dim(dprob_all, first_row, own_rows, 0)
    route_mine = lax.dynamic_slice_in_dim(route_b, first_row, own_rows, 0)
    sigma_mine = lax.dynamic_slice_in_dim(sigma_b, first_row, own_rows, 0)
    onehot_mine = lax.dynamic_slice_in_dim(onehot_b, first_row, own_rows, 0)
    slope = route_mine * dprob_mine * sigma_mine * (1.0 - sigma_mine)
    router_wide = w_router.astype(jnp.float32)
    spread = router_wide[:, 0][None, :] - jnp.dot(
        onehot_mine, router_wide.T, precision=lax.Precision.HIGHEST
    )
    dnormed = slope[:, None] * spread
    scaled_rows = dnormed * gain.astype(jnp.float32)
    normalized_input = backward_wide_rows * backward_inverse_norm
    norm_input_gradient = backward_inverse_norm * (
        scaled_rows
        - normalized_input * jnp.mean(scaled_rows * normalized_input, axis=-1, keepdims=True)
    )
    input_grad = (grad_out.astype(jnp.float32) + norm_input_gradient).astype(jnp.bfloat16)
    fwd_in = from_behind(layer_out, "section", 1)
    incoming_gradient = from_behind(input_grad, "section", -1)
    return (fwd_in[None], incoming_gradient[None], dact[None])


def solution(mesh):
    placed = (
        P("section", "et", None),
        P("section", None, "et"),
        P("section", None, None),
        P("section", "et", None),
        P("section", None, "et"),
        P("section", None, None),
        P("section", "et", None),
        P("section", None),
        P("section", None, None),
        P("section", "et", None),
    )
    return jax.shard_map(
        shards,
        mesh=mesh,
        in_specs=placed,
        out_specs=(P("section", "et", None), P("section", "et", None), P("section", None, "et")),
        check_vma=False,
    )
```

profile of v0, /device:TPU:6, one launch (start us, length us, event | category | flops | bytes accessed | tf_op | source)
XLA Modules:
  0.0 256.7 jit_solution(1746351903962819599)
XLA Ops:
  7.2 0.9 convert_reduce_fusion.5
  8.1 1.4 convert_reduce_fusion
  11.9 1.4 scatter_custom_fusion
  14.1 1.0 fusion.22
  15.1 1.1 fusion.6
  16.3 17.6 %all-gather.1 = bf16[16,16,8]{1,2,0:T(8,128)(2,1)S(1)} all-gather(bf16[1,16,8]{1,2,0:T(8,128)(2,1)S(1)} %fusion.6), channel_id=1, replica_groups=mesh['section'=32,'et'=16] {'et'}, dimensions={0}, use_global_device_ids=true | all-gather | bytes 4352 | tf_op jit(solution)/shard_map/all_gather | solution.py:69
  34.1 1.9 gather_fusion
  36.0 1.3 gather_fusion.1
  37.3 1.5 fusion
  40.4 1.0 fusion.7
  42.6 1.2 compare_select_fusion
  43.8 1.4 scatter_custom_fusion.1
  45.9 15.0 %all-gather.2 = bf16[16,16,8]{1,2,0:T(8,128)(2,1)S(1)} all-gather(bf16[1,16,8]{1,2,0:T(8,128)(2,1)S(1)} %fusion.7), channel_id=1, replica_groups=mesh['section'=32,'et'=16] {'et'}, dimensions={0}, use_global_device_ids=true | all-gather | bytes 4352 | tf_op jit(solution)/shard_map/all_gather | solution.py:70
  63.9 1.4 slice_convert_fusion
  65.3 92.2 %all-reduce.2.cloned.1.call-done = bf16[128,3072]{1,0:T(8,128)(2,1)} async-done(((bf16[128,3072]{1,0:T(8,128)(2,1)}), bf16[128,3072]{1,0:T(8,128)(2,1)}) %all-reduce.2.cloned.1.call-update) | async-done | bytes 786448 | tf_op jit(solution)/shard_map/psum | solution.py:80
  157.6 2.4 convert_element_type.106
  160.0 2.2 gather_fusion.2
  162.2 0.8 fusion.23
  163.0 3.5 %collective-permute-start = (bf16[16,3072]{1,0:T(8,128)(2,1)S(1)}, bf16[16,3072]{1,0:T(8,128)(2,1)}, u32[]{:S(2)}, u32[]{:S(2)}) collective-permute-start(bf16[16,3072]{1,0:T(8,128)(2,1)S(1)} %fusion.23), channel_id=1, source_target_pairs={{0,16},{16,32},{32,48},{48,64},{64,80},{80,96},{96,112},{112,128},... | collective-permute-start | bytes 294920 | tf_op jit(solution)/shard_map/ppermute | solution.py:10
  167.2 2.4 collective-permute-done
  169.6 32.3 %all-gather.5.cloned.1.call-done = bf16[1,256,3072]{2,1,0:T(8,128)(2,1)} async-done(((bf16[1,16,3072]{2,1,0:T(8,128)(2,1)}), bf16[1,256,3072]{2,1,0:T(8,128)(2,1)}) %all-gather.5.cloned.1.call-update) | async-done | bytes 1572880 | tf_op jit(solution)/shard_map/all_gather | solution.py:71
  201.9 4.5 %gather_fusion.3 = bf16[128,3072]{1,0:T(8,128)(2,1)} fusion(bf16[256,3072]{1,0:T(8,128)(2,1)} %bitcast.108, s32[1024]{0:T(1024)} %pad_clamp_fusion.1), kind=kCustom, calls=%fused_computation.3 | custom fusion | bytes 1573376 | tf_op jit(solution)/shard_map/gather | solution.py:89
  206.3 2.3 fusion.3
  208.7 1.8 gather_fusion.4
  210.5 1.3 fusion.8
  211.8 24.9 %psum.15 = f32[256]{0:T(256)S(1)} all-reduce(f32[256]{0:T(256)S(1)} %fusion.8), channel_id=1, replica_groups=mesh['section'=32,'et'=16] {'et'}, use_global_device_ids=true, to_apply=%region_22.23 | all-reduce | flops 256 | bytes 2048 | tf_op jit(solution)/shard_map/psum | solution.py:94
  236.8 1.2 fusion.17
  238.0 1.0 fusion.21
  239.0 2.8 %collective-permute-start.1 = (bf16[16,3072]{1,0:T(8,128)(2,1)S(1)}, bf16[16,3072]{1,0:T(8,128)(2,1)S(1)}, u32[]{:S(2)}, u32[]{:S(2)}) collective-permute-start(bf16[16,3072]{1,0:T(8,128)(2,1)S(1)} %fusion.21), channel_id=1, source_target_pairs={{16,0},{32,16},{48,32},{64,48},{80,64},{96,80},{112,96},{128,112},... | collective-permute-start | bytes 294920 | tf_op jit(solution)/shard_map/ppermute | solution.py:10
  241.8 1.9 fusion.10
  243.7 4.0 %collective-permute-done.1 = bf16[16,3072]{1,0:T(8,128)(2,1)S(1)} collective-permute-done((bf16[16,3072]{1,0:T(8,128)(2,1)S(1)}, bf16[16,3072]{1,0:T(8,128)(2,1)S(1)}, u32[]{:S(2)}, u32[]{:S(2)}) %collective-permute-start.1) | collective-permute-done | bytes 98336 | tf_op jit(solution)/shard_map/ppermute | solution.py:10
  247.6 1.5 copy.20
  (79 shorter events, 11.3 us)
Async XLA Ops:
  7.2 30.1 %copy-start = (bf16[1,512,3072]{2,1,0:T(8,128)(2,1)S(1)}, bf16[1,512,3072]{2,1,0:T(8,128)(2,1)}, u32[]{:S(2)}) copy-start(bf16[1,512,3072]{2,1,0:T(8,128)(2,1)} %param.19) | copy-start | bytes 9437188
  7.2 150.4 %all-reduce.2.cloned.1.call-start = ((), (), s32[]{:S(2)}) async-start(), calls=%async_computation | async-start | bytes 1572864 | tf_op jit(solution)/shard_map/psum | solution.py:80
  34.0 6.2 %copy-start.2 = (bf16[1,16,3072]{2,1,0:T(8,128)(2,1)S(1)}, bf16[1,16,3072]{2,1,0:T(8,128)(2,1)}, u32[]{:S(2)}) copy-start(bf16[1,16,3072]{2,1,0:T(8,128)(2,1)} %param.13) | copy-start | bytes 294916
  35.9 25.7 %copy-start.4 = (s32[1,256,2]{1,2,0:T(2,128)S(1)}, s32[1,256,2]{1,2,0:T(2,128)}, u32[]{:S(2)}) copy-start(s32[1,256,2]{1,2,0:T(2,128)} %param.15) | copy-start | bytes 6148
  38.8 123.5 %copy-start.1 = (bf16[1,16,3072]{2,1,0:T(8,128)(2,1)S(1)}, bf16[1,16,3072]{2,1,0:T(8,128)(2,1)}, u32[]{:S(2)}) copy-start(bf16[1,16,3072]{2,1,0:T(8,128)(2,1)} %param.10) | copy-start | bytes 294916
  38.8 163.1 %all-gather.5.cloned.1.call-start = ((), (), s32[]{:S(2)}) async-start(), calls=%async_computation.1 | async-start | bytes 1671168 | tf_op jit(solution)/shard_map/all_gather | solution.py:71
  40.4 1.0 copy-start.9
  163.0 6.6 %collective-permute-start = (bf16[16,3072]{1,0:T(8,128)(2,1)S(1)}, bf16[16,3072]{1,0:T(8,128)(2,1)}, u32[]{:S(2)}, u32[]{:S(2)}) collective-permute-start(bf16[16,3072]{1,0:T(8,128)(2,1)S(1)} %fusion.23), channel_id=1, source_target_pairs={{0,16},{16,32},{32,48},{48,64},{64,80},{80,96},{96,112},{112,128},... | collective-permute-start | bytes 294920 | tf_op jit(solution)/shard_map/ppermute | solution.py:10
  208.7 1.8 copy-start.8
  208.7 28.0 %copy-start.6 = (f32[256]{0:T(256)S(1)}, f32[256]{0:T(256)}, u32[]{:S(2)}) copy-start(f32[256]{0:T(256)} %add_divide_fusion) | copy-start | bytes 3076
  208.7 28.1 %copy-start.3 = (f32[3072,1]{0,1:T(1,128)S(1)}, f32[3072,1]{0,1:T(1,128)}, u32[]{:S(2)}) copy-start(f32[3072,1]{0,1:T(1,128)} %slice_convert_fusion) | copy-start | bytes 36868
  208.7 28.1 %copy-start.7 = (pred[256,8]{0,1:T(8,128)(4,1)S(1)}, pred[256,8]{0,1:T(8,128)(4,1)}, u32[]{:S(2)}) copy-start(pred[256,8]{0,1:T(8,128)(4,1)} %iota_compare_fusion) | copy-start | bytes 6148
  208.7 33.1 %copy-start.5 = (f32[256,1]{0,1:T(1,128)S(1)}, f32[256,1]{0,1:T(1,128)}, u32[]{:S(2)}) copy-start(f32[256,1]{0,1:T(1,128)} %get-tuple-element.14) | copy-start | bytes 3076
  239.0 8.6 %collective-permute-start.1 = (bf16[16,3072]{1,0:T(8,128)(2,1)S(1)}, bf16[16,3072]{1,0:T(8,128)(2,1)S(1)}, u32[]{:S(2)}, u32[]{:S(2)}) collective-permute-start(bf16[16,3072]{1,0:T(8,128)(2,1)S(1)} %fusion.21), channel_id=1, source_target_pairs={{16,0},{32,16},{48,32},{64,48},{80,64},{96,80},{112,96},{128,112},... | collective-permute-start | bytes 294920 | tf_op jit(solution)/shard_map/ppermute | solution.py:10
Sparse Core Ops, SparseCore 0:
  38.9 118.5 all-reduce.1
  159.7 42.1 all-gather.4
where the time goes:
time: 257 us
  waiting for transfers between devices  132 us (51%)
  blocking collectives  57.5 us (22%)
  other arithmetic  22.1 us (9%)
  local copies, waits for them, and re-layouts  17.6 us (7%)
  between operations  14.3 us (6%)
  matrix products  7.15 us (3%)
  starting transfers between devices  6.38 us (2%)
    psum x1, waiting for transfers between devices, shards(): summed = lax.psum(compact.astype(jnp.bfloat16), 'et').astype(jnp.float32)  92.2 us
    all_gather x1, waiting for transfers between devices, shards(): lax.all_gather(grad_out, 'et', axis=0, tiled=True)  32.3 us
    psum x1, blocking collectives, shards(): dprob_all = lax.psum(dprob_part, 'et')  24.9 us
    all_gather x1, blocking collectives, shards(): lax.all_gather(logit_f, 'et', axis=0, tiled=True)  17.6 us
    all_gather x1, blocking collectives, shards(): lax.all_gather(logit_b, 'et', axis=0, tiled=True)  15 us
    ppermute x2, waiting for transfers between devices, from_behind(): lax.ppermute(value, axis, [(source, source + steps) for source in range(f...  6.38 us
    ppermute x2, starting transfers between devices, from_behind(): lax.ppermute(value, axis, [(source, source + steps) for source in range(f...  6.3 us
  transfers between devices with their start and end apart: 4, of which 4 were waited for; matrix products, arithmetic and copies ran while one was open for 7% of the time, Pallas kernels for 0%

commit v1 on v0

--- a/solution.py
+++ b/solution.py
@@ -91,7 +91,11 @@
     back_up = spread_back(up_compact, member_b, place_b, capacity)
     dact = (backward_coefficient[:, None] * back_up).astype(jnp.bfloat16)
     dprob_part = jnp.sum(act_bwd.astype(jnp.float32) * back_up, axis=1)
-    dprob_all = lax.psum(dprob_part, "et")
+    dprob_all = dprob_part
+    devs = lax.psum(1, "et")
+    for rr in [at for at in (1, 2, 4, 8, 16) if at < devs]:
+        fresh = lax.ppermute(dprob_all, "et", [(u, u ^ rr) for u in range(devs)])
+        dprob_all = dprob_all + fresh
     dprob_mine = lax.dynamic_slice_in_dim(dprob_all, first_row, own_rows, 0)
     route_mine = lax.dynamic_slice_in_dim(route_b, first_row, own_rows, 0)
     sigma_mine = lax.dynamic_slice_in_dim(sigma_b, first_row, own_rows, 0)

time: 257 us -> 218 us (0.85)
  waiting for transfers between devices: 132 us -> 103 us
  blocking collectives: 57.5 us -> 32.7 us
  starting transfers between devices: 6.38 us -> 20.2 us
    all_gather x1, waiting for transfers between devices: 32.3 us -> 0.01 us  [shards(): lax.all_gather(grad_out, 'et', axis=0, tiled=True)]
    psum x1 -> x0, blocking collectives: 24.9 us -> none  [shards(): dprob_all = lax.psum(dprob_part, 'et')]
    ppermute x0 -> x4, starting transfers between devices: none -> 14.3 us  [shards(): fresh = lax.ppermute(dprob_all, 'et', [(u, u ^ rr) for u in range(devs)])]
    psum x1, waiting for transfers between devices: 92.2 us -> 95.1 us  [shards(): summed = lax.psum(compact.astype(jnp.bfloat16), 'et').astype(jnp.float32)]
  transfers between devices with their start and end apart: 4 -> 8, of which waited for: 4 -> 3; matrix products, arithmetic and copies ran while one was open for 7% -> 19% of each run, Pallas kernels for 0% -> 0%
where the time goes in v1:
time: 218 us; the launch traced here: 216 us
  waiting for transfers between devices  103 us (47%)
  blocking collectives  32.7 us (15%)
  other arithmetic  22.8 us (10%)
  starting transfers between devices  20.2 us (9%)
  local copies, waits for them, and re-layouts  16.6 us (8%)
  between operations  14.4 us (7%)
  matrix products  6.5 us (3%)
    psum x1, waiting for transfers between devices, shards(): summed = lax.psum(compact.astype(jnp.bfloat16), 'et').astype(jnp.float32)  95.1 us
    all_gather x1, blocking collectives, shards(): lax.all_gather(logit_f, 'et', axis=0, tiled=True)  17.6 us
    all_gather x1, blocking collectives, shards(): lax.all_gather(logit_b, 'et', axis=0, tiled=True)  15 us
    ppermute x4, starting transfers between devices, shards(): fresh = lax.ppermute(dprob_all, 'et', [(u, u ^ rr) for u in range(devs)])  14.3 us
    ppermute x2, starting transfers between devices, from_behind(): lax.ppermute(value, axis, [(source, source + steps) for source in range(f...  5.84 us
    ppermute x2, waiting for transfers between devices, from_behind(): lax.ppermute(value, axis, [(source, source + steps) for source in range(f...  4.42 us
  transfers between devices with their start and end apart: 8, of which 3 were waited for; matrix products, arithmetic and copies ran while one was open for 19% of the time, Pallas kernels for 0%

profile of v1, /device:TPU:6, one launch (start us, length us, event | category | flops | bytes accessed | tf_op | source)
XLA Modules:
  0.0 215.7 jit_solution(10610477418814259614)
XLA Ops:
  8.0 1.5 convert_reduce_fusion
  11.0 1.0 fusion.22
  12.1 1.1 fusion.6
  13.2 17.6 %all-gather.1 = bf16[16,16,8]{1,2,0:T(8,128)(2,1)S(1)} all-gather(bf16[1,16,8]{1,2,0:T(8,128)(2,1)S(1)} %fusion.6), channel_id=1, replica_groups=mesh['section'=32,'et'=16] {'et'}, dimensions={0}, use_global_device_ids=true | all-gather | bytes 4352 | tf_op jit(solution)/shard_map/all_gather | solution.py:69
  31.2 0.7 compare_select_fusion.8
  32.6 1.4 scatter_custom_fusion
  34.0 1.9 gather_fusion
  36.7 1.3 gather_fusion.1
  38.0 1.5 fusion
  41.6 15.0 %all-gather.2 = bf16[16,16,8]{1,2,0:T(8,128)(2,1)S(1)} all-gather(bf16[1,16,8]{1,2,0:T(8,128)(2,1)S(1)} %fusion.7), channel_id=1, replica_groups=mesh['section'=32,'et'=16] {'et'}, dimensions={0}, use_global_device_ids=true | all-gather | bytes 4352 | tf_op jit(solution)/shard_map/all_gather | solution.py:70
  58.7 1.4 scatter_custom_fusion.1
  61.4 4.3 %gather_fusion.3 = bf16[128,3072]{1,0:T(8,128)(2,1)} fusion(bf16[256,3072]{1,0:T(8,128)(2,1)} %bitcast.108, s32[1024]{0:T(1024)S(1)} %pad_clamp_fusion.1), kind=kCustom, calls=%fused_computation.3 | custom fusion | bytes 1573376 | tf_op jit(solution)/shard_map/gather | solution.py:89
  65.7 2.3 %fusion.3 = f32[128,512]{1,0:T(8,128)S(1)} fusion(bf16[128,3072]{1,0:T(8,128)(2,1)} %gather_fusion.3, bf16[1,512,3072]{2,1,0:T(8,128)(2,1)S(1)} %copy-done), kind=kOutput, calls=%fused_computation.12 | convolution fusion | flops 402653184 | bytes 4194304 | tf_op jit(solution)/shard_map/dot_general | solution.py:88
  68.0 1.8 gather_fusion.4
  69.8 1.4 fusion.8
  71.1 2.3 %collective-permute-start.1 = (f32[256]{0:T(256)S(1)}, f32[256]{0:T(256)S(1)}, u32[]{:S(2)}, u32[]{:S(2)}) collective-permute-start(f32[256]{0:T(256)S(1)} %fusion.8), channel_id=1, source_target_pairs={{0,1},{1,0},{2,3},{3,2},{4,5},{5,4},{6,7},{7,6},{8,9},{9,8},{10,11... | collective-permute-start | bytes 3080 | tf_op jit(solution)/shard_map/ppermute | solution.py:97
  73.4 1.3 pad_clamp_fusion.2
  75.3 3.1 %collective-permute-start.2 = (f32[256]{0:T(256)}, f32[256]{0:T(256)}, u32[]{:S(2)}, u32[]{:S(2)}) collective-permute-start(f32[256]{0:T(256)} %add.148), channel_id=1, source_target_pairs={{0,2},{1,3},{2,0},{3,1},{4,6},{5,7},{6,4},{7,5},{8,10},{9,11},{10,... | collective-permute-start | bytes 3080 | tf_op jit(solution)/shard_map/ppermute | solution.py:97
  79.0 95.1 %all-reduce.2.cloned.1.call-done = bf16[128,3072]{1,0:T(8,128)(2,1)} async-done(((bf16[128,3072]{1,0:T(8,128)(2,1)}), bf16[128,3072]{1,0:T(8,128)(2,1)}) %all-reduce.2.cloned.1.call-update) | async-done | bytes 786448 | tf_op jit(solution)/shard_map/psum | solution.py:80
  174.2 2.4 %convert_element_type.106 = f32[128,3072]{1,0:T(8,128)} convert(bf16[128,3072]{1,0:T(8,128)(2,1)} %all-reduce.2.cloned.1.call-done) | non-fusion elementwise | flops 393216 | bytes 2359296 | tf_op jit(solution)/shard_map/convert_element_type | solution.py:80
  176.6 2.2 %gather_fusion.2 = f32[16,3072]{1,0:T(8,128)S(1)} fusion(f32[128,3072]{1,0:T(8,128)} %convert_element_type.106, s32[1024]{0:T(1024)} %pad_clamp_fusion.2), kind=kCustom, calls=%fused_computation.2 | custom fusion | bytes 393280 | tf_op jit(solution)/shard_map/gather | solution.py:43
  179.5 2.6 %collective-permute-start.3 = (f32[256]{0:T(256)S(1)}, f32[256]{0:T(256)S(1)}, u32[]{:S(2)}, u32[]{:S(2)}) collective-permute-start(f32[256]{0:T(256)S(1)} %add.149), channel_id=1, source_target_pairs={{0,4},{1,5},{2,6},{3,7},{4,0},{5,1},{6,2},{7,3},{8,12},{9,13},{10,... | collective-permute-start | bytes 3080 | tf_op jit(solution)/shard_map/ppermute | solution.py:97
  182.1 0.8 fusion.23
  182.9 3.5 %collective-permute-start = (bf16[16,3072]{1,0:T(8,128)(2,1)S(1)}, bf16[16,3072]{1,0:T(8,128)(2,1)S(1)}, u32[]{:S(2)}, u32[]{:S(2)}) collective-permute-start(bf16[16,3072]{1,0:T(8,128)(2,1)S(1)} %fusion.23), channel_id=1, source_target_pairs={{0,16},{16,32},{32,48},{48,64},{64,80},{80,96},{96,112},{112,128},... | collective-permute-start | bytes 294920 | tf_op jit(solution)/shard_map/ppermute | solution.py:10
  186.5 6.4 %collective-permute-start.4 = (f32[256]{0:T(256)S(1)}, f32[256]{0:T(256)S(1)}, u32[]{:S(2)}, u32[]{:S(2)}) collective-permute-start(f32[256]{0:T(256)S(1)} %add.150), channel_id=1, source_target_pairs={{0,8},{1,9},{2,10},{3,11},{4,12},{5,13},{6,14},{7,15},{8,0},{9,1},... | collective-permute-start | bytes 3080 | tf_op jit(solution)/shard_map/ppermute | solution.py:97
  193.5 2.3 %collective-permute-done.4 = f32[256]{0:T(256)S(1)} collective-permute-done((f32[256]{0:T(256)S(1)}, f32[256]{0:T(256)S(1)}, u32[]{:S(2)}, u32[]{:S(2)}) %collective-permute-start.4) | collective-permute-done | bytes 1056 | tf_op jit(solution)/shard_map/ppermute | solution.py:97
  195.8 0.7 subtract_multiply_fusion
  196.6 1.4 fusion.17
  197.9 1.0 fusion.21
  199.0 2.3 %collective-permute-start.5 = (bf16[16,3072]{1,0:T(8,128)(2,1)S(1)}, bf16[16,3072]{1,0:T(8,128)(2,1)S(1)}, u32[]{:S(2)}, u32[]{:S(2)}) collective-permute-start(bf16[16,3072]{1,0:T(8,128)(2,1)S(1)} %fusion.21), channel_id=1, source_target_pairs={{16,0},{32,16},{48,32},{64,48},{80,64},{96,80},{112,96},{128,112},... | collective-permute-start | bytes 294920 | tf_op jit(solution)/shard_map/ppermute | solution.py:10
  201.3 1.9 fusion.10
  203.2 4.4 %collective-permute-done.5 = bf16[16,3072]{1,0:T(8,128)(2,1)S(1)} collective-permute-done((bf16[16,3072]{1,0:T(8,128)(2,1)S(1)}, bf16[16,3072]{1,0:T(8,128)(2,1)S(1)}, u32[]{:S(2)}, u32[]{:S(2)}) %collective-permute-start.5) | collective-permute-done | bytes 98336 | tf_op jit(solution)/shard_map/ppermute | solution.py:10
  (88 shorter events, 13.4 us)
Async XLA Ops:
  7.2 30.8 %copy-start = (bf16[1,512,3072]{2,1,0:T(8,128)(2,1)S(1)}, bf16[1,512,3072]{2,1,0:T(8,128)(2,1)}, u32[]{:S(2)}) copy-start(bf16[1,512,3072]{2,1,0:T(8,128)(2,1)} %param.19) | copy-start | bytes 9437188
  7.2 54.2 %all-gather.5.cloned.1.call-start = ((), (), s32[]{:S(2)}) async-start(), calls=%async_computation.1 | async-start | bytes 1671168 | tf_op jit(solution)/shard_map/all_gather | solution.py:71
  7.9 166.2 %all-reduce.2.cloned.1.call-start = ((), (), s32[]{:S(2)}) async-start(), calls=%async_computation | async-start | bytes 1572864 | tf_op jit(solution)/shard_map/psum | solution.py:80
  34.0 5.5 %copy-start.5 = (s32[1,256,2]{1,2,0:T(2,128)S(1)}, s32[1,256,2]{1,2,0:T(2,128)}, u32[]{:S(2)}) copy-start(s32[1,256,2]{1,2,0:T(2,128)} %param.15) | copy-start | bytes 6148
  34.0 6.1 %copy-start.3 = (bf16[1,16,3072]{2,1,0:T(8,128)(2,1)S(1)}, bf16[1,16,3072]{2,1,0:T(8,128)(2,1)}, u32[]{:S(2)}) copy-start(bf16[1,16,3072]{2,1,0:T(8,128)(2,1)} %param.13) | copy-start | bytes 294916
  34.0 6.8 %copy-start.7 = (bf16[1,3072,8]{1,2,0:T(8,128)(2,1)S(1)}, bf16[1,3072,8]{1,2,0:T(8,128)(2,1)}, u32[]{:S(2)}) copy-start(bf16[1,3072,8]{1,2,0:T(8,128)(2,1)} %param.18) | copy-start | bytes 147460
  39.5 21.8 %copy-start.6 = (f32[256]{0:T(256)}, f32[256]{0:T(256)S(1)}, u32[]{:S(2)}) copy-start(f32[256]{0:T(256)S(1)} %convert_reduce_fusion.4) | copy-start | bytes 3076
  40.2 21.1 %copy-start.8 = (f32[16]{0:T(128)}, f32[16]{0:T(128)S(1)}, u32[]{:S(2)}) copy-start(f32[16]{0:T(128)S(1)} %add_rsqrt_fusion) | copy-start | bytes 196
  56.8 4.6 %copy-start.4 = (f32[256]{0:T(256)}, f32[256]{0:T(256)S(1)}, u32[]{:S(2)}) copy-start(f32[256]{0:T(256)S(1)} %select_reduce_fusion) | copy-start | bytes 3076
  69.8 112.4 %copy-start.1 = (bf16[1,16,3072]{2,1,0:T(8,128)(2,1)S(1)}, bf16[1,16,3072]{2,1,0:T(8,128)(2,1)}, u32[]{:S(2)}) copy-start(bf16[1,16,3072]{2,1,0:T(8,128)(2,1)} %param.10) | copy-start | bytes 294916
  69.8 128.2 %copy-start.2 = (bf16[1,16,3072]{2,1,0:T(8,128)(2,1)S(1)}, bf16[1,16,3072]{2,1,0:T(8,128)(2,1)}, u32[]{:S(2)}) copy-start(bf16[1,16,3072]{2,1,0:T(8,128)(2,1)} %param.16) | copy-start | bytes 294916
  71.1 3.5 %collective-permute-start.1 = (f32[256]{0:T(256)S(1)}, f32[256]{0:T(256)S(1)}, u32[]{:S(2)}, u32[]{:S(2)}) collective-permute-start(f32[256]{0:T(256)S(1)} %fusion.8), channel_id=1, source_target_pairs={{0,1},{1,0},{2,3},{3,2},{4,5},{5,4},{6,7},{7,6},{8,9},{9,8},{10,11... | collective-permute-start | bytes 3080 | tf_op jit(solution)/shard_map/ppermute | solution.py:97
  75.3 103.6 %collective-permute-start.2 = (f32[256]{0:T(256)}, f32[256]{0:T(256)}, u32[]{:S(2)}, u32[]{:S(2)}) collective-permute-start(f32[256]{0:T(256)} %add.148), channel_id=1, source_target_pairs={{0,2},{1,3},{2,0},{3,1},{4,6},{5,7},{6,4},{7,5},{8,10},{9,11},{10,... | collective-permute-start | bytes 3080 | tf_op jit(solution)/shard_map/ppermute | solution.py:97
  179.5 6.9 %collective-permute-start.3 = (f32[256]{0:T(256)S(1)}, f32[256]{0:T(256)S(1)}, u32[]{:S(2)}, u32[]{:S(2)}) collective-permute-start(f32[256]{0:T(256)S(1)} %add.149), channel_id=1, source_target_pairs={{0,4},{1,5},{2,6},{3,7},{4,0},{5,1},{6,2},{7,3},{8,12},{9,13},{10,... | collective-permute-start | bytes 3080 | tf_op jit(solution)/shard_map/ppermute | solution.py:97
  182.9 10.6 %collective-permute-start = (bf16[16,3072]{1,0:T(8,128)(2,1)S(1)}, bf16[16,3072]{1,0:T(8,128)(2,1)S(1)}, u32[]{:S(2)}, u32[]{:S(2)}) collective-permute-start(bf16[16,3072]{1,0:T(8,128)(2,1)S(1)} %fusion.23), channel_id=1, source_target_pairs={{0,16},{16,32},{32,48},{48,64},{64,80},{80,96},{96,112},{112,128},... | collective-permute-start | bytes 294920 | tf_op jit(solution)/shard_map/ppermute | solution.py:10
  186.5 9.4 %collective-permute-start.4 = (f32[256]{0:T(256)S(1)}, f32[256]{0:T(256)S(1)}, u32[]{:S(2)}, u32[]{:S(2)}) collective-permute-start(f32[256]{0:T(256)S(1)} %add.150), channel_id=1, source_target_pairs={{0,8},{1,9},{2,10},{3,11},{4,12},{5,13},{6,14},{7,15},{8,0},{9,1},... | collective-permute-start | bytes 3080 | tf_op jit(solution)/shard_map/ppermute | solution.py:97
  199.0 8.6 %collective-permute-start.5 = (bf16[16,3072]{1,0:T(8,128)(2,1)S(1)}, bf16[16,3072]{1,0:T(8,128)(2,1)S(1)}, u32[]{:S(2)}, u32[]{:S(2)}) collective-permute-start(bf16[16,3072]{1,0:T(8,128)(2,1)S(1)} %fusion.21), channel_id=1, source_target_pairs={{16,0},{32,16},{48,32},{64,48},{80,64},{96,80},{112,96},{128,112},... | collective-permute-start | bytes 294920 | tf_op jit(solution)/shard_map/ppermute | solution.py:10
Sparse Core Ops, SparseCore 0:
  10.1 45.9 all-gather.4
  58.4 115.7 all-reduce.1
